TPU v7x, 512 devices: a whole 4x8x8 slice. The times are simulated.
512 devices in a mesh: ind: 64 (over y, z), snp: 8 (over x, core).
Axes of the slice: x: 4, y: 8, z: 8, core: 2. Of those that a mesh axis runs over, the one named last changes fastest.
Arguments:
- genotypes: int32 [4096, 16384], P('ind', 'snp'), may hold values from 0 to 2
- observed: int32 [4096, 16384], P('ind', 'snp'), may hold values from 0 to 1
- ancestry: float32 [4096, 32], P('ind'), may hold values from 0.018 to 54.6, as said below
- freqs: float32 [16384, 32], P(('snp', 'ind')), may hold values from 0.05 to 0.95
Outputs:
- ancestry_out: float32 [4096, 32], P('ind')
- freqs_out: float32 [16384, 32], P(('snp', 'ind'))
Inputs may be any that keep to these rules, and one draw needn't show every extreme that they name: `ancestry`: positive weights.
All inputs are finite; a program needn't handle non-finite values.
Results may differ from a plain program's by a relative error of at most 0.0003.
Values sent between devices are 32-bit elements; how exact they have to be, the bound alone decides.
No kernel may reach another device: no remote copies, remote signals or barrier semaphores. Data moves between devices by JAX's collectives and lax.ppermute only.
A program may use at most 64 MiB of HBM per device.

v0:
```python
import jax
import jax.numpy as jnp
from jax import lax
from jax.sharding import Mesh
from jax.sharding import PartitionSpec as P

STEPS = 3
clip_low = 1e-05
high = lax.Precision.HIGHEST
IND_AXES = ("yh", "yl", "z")
SNP_AXES = ("x", "c")
ROW_GROUP = ("yl", "z")
COL_GROUP = ("c", "x", "yh")


def doubling_sum(value, axes):
    for name in axes:
        size = lax.axis_size(name)
        step = 1
        while step < size:
            pairs = [(j, j ^ step) for j in range(size)]
            value = value + lax.ppermute(value, name, pairs)
            step *= 2
    return value


def per_device(genotypes, observed, ancestry, freqs):
    quarter = lax.axis_size("yh")
    geno = genotypes.astype(jnp.float32)
    seen = observed.astype(jnp.float32)
    counts = jnp.stack([seen * geno, seen * (2.0 - geno)])
    counts = lax.all_to_all(counts, "yh", 2, 1, tiled=True)
    hits, misses = (counts[0], counts[1])
    own_rows = ancestry.shape[0]
    own_snps = freqs.shape[0]
    q_own = ancestry / jnp.sum(ancestry, axis=1, keepdims=True)
    q_zero = lax.all_gather(q_own, "yh", axis=0, tiled=True)
    f_zero = lax.all_gather(freqs, ROW_GROUP, axis=0, tiled=True)

    def em_map(q_rows, f_state):
        prob = jnp.dot(q_rows, f_state.T, precision=high, preferred_element_type=jnp.float32)
        ratio_a = hits / prob
        ratio_b = misses / (1.0 - prob)
        sum_a = jnp.dot(ratio_a, f_state, precision=high, preferred_element_type=jnp.float32)
        sum_b = jnp.dot(ratio_b, 1.0 - f_state, precision=high, preferred_element_type=jnp.float32)
        c_part = lax.dot_general(
            ratio_a,
            q_rows,
            (((0,), (0,)), ((), ())),
            precision=high,
            preferred_element_type=jnp.float32,
        )
        d_part = lax.dot_general(
            ratio_b,
            q_rows,
            (((0,), (0,)), ((), ())),
            precision=high,
            preferred_element_type=jnp.float32,
        )
        q_sum = doubling_sum(sum_a + sum_b, COL_GROUP)
        cd_total = doubling_sum(jnp.concatenate([c_part, d_part], axis=1), ROW_GROUP)
        q_next = q_rows * q_sum
        q_next = q_next / jnp.sum(q_next, axis=1, keepdims=True)
        width = f_state.shape[1]
        c_total, d_total = (cd_total[:, :width], cd_total[:, width:])
        f_next = f_state * c_total / (f_state * c_total + (1.0 - f_state) * d_total)
        return (q_next, f_next)

    for step in range(STEPS):
        q_one, f_one = em_map(q_zero, f_zero)
        q_two, f_two = em_map(q_one, f_one)
        rq = q_one - q_zero
        rf = f_one - f_zero
        vq = q_two - 2.0 * q_one + q_zero
        vf = f_two - 2.0 * f_one + f_zero
        q_parts = doubling_sum(jnp.stack([jnp.sum(rq * rq), jnp.sum(vq * vq)]), ROW_GROUP)
        f_parts = doubling_sum(jnp.stack([jnp.sum(rf * rf), jnp.sum(vf * vf)]), COL_GROUP)
        first = q_parts[0] + f_parts[0]
        second = q_parts[1] + f_parts[1]
        alpha = -jnp.sqrt(first / (second + 1e-20))
        q_ext = jnp.clip(q_zero - 2.0 * alpha * rq + alpha * alpha * vq, clip_low, 1.0 - clip_low)
        q_zero = q_ext / jnp.sum(q_ext, axis=1, keepdims=True)
        f_zero = jnp.clip(f_zero - 2.0 * alpha * rf + alpha * alpha * vf, clip_low, 1.0 - clip_low)
    q_final = lax.dynamic_slice_in_dim(q_zero, lax.axis_index("yh") * own_rows, own_rows, 0)
    f_index = lax.axis_index("yl") * lax.axis_size("z") + lax.axis_index("z")
    f_final = lax.dynamic_slice_in_dim(f_zero, f_index * own_snps, own_snps, 0)
    del quarter
    return (q_final, f_final)


def solution(mesh):
    ind_size = mesh.shape["ind"]
    snp_size = mesh.shape["snp"]
    quarter = 4
    lanes = ind_size // quarter
    view = Mesh(
        mesh.devices.reshape(quarter, 2, lanes // 2, snp_size // 2, 2), ("yh", "yl", "z", "x", "c")
    )
    in_specs = (
        P(IND_AXES, SNP_AXES),
        P(IND_AXES, SNP_AXES),
        P(IND_AXES, None),
        P(SNP_AXES + IND_AXES, None),
    )
    out_specs = (P(IND_AXES, None), P(SNP_AXES + IND_AXES, None))
    return jax.shard_map(
        per_device, mesh=view, in_specs=in_specs, out_specs=out_specs, check_vma=False
    )
```

profile of v0, /device:TPU:56, one launch (start us, length us, event | category | flops | bytes accessed | tf_op | source)
XLA Modules:
  0.0 610.7 jit_solution(14223782295887713590)
XLA Ops:
  9.1 7.0 %all-to-all-start = ((f32[4,1,65536]{2,1,0:T(1,128)}), f32[4,1,65536]{2,1,0:T(1,128)S(1)}, u32[]{:S(2)}, u32[]{:S(2)}) async-start(f32[4,1,65536]{2,1,0:T(1,128)} %reshape.50), calls=%async_computation | async-start | bytes 2097152 | tf_op jit(solution)/shard_map/all_to_all | solution.py:32
  16.1 32.8 %all-gather = f32[4,64,32]{1,2,0:T(8,128)S(1)} all-gather(f32[1,64,32]{1,2,0:T(8,128)S(1)} %divide_bitcast_fusion), channel_id=1, replica_groups=mesh['yh'=4,'yl'=2,'z'=8,'x'=4,'c'=2] {'yh'}, dimensions={0}, use_global_device_ids=true | all-gather | bytes 40960 | tf_op jit(solution)/shard_map/all_gather | solution.py:37
  49.1 40.7 %all_gather.7 = f32[512,32]{1,0:T(8,128)S(1)} all-gather(f32[32,32]{1,0:T(8,128)S(1)} %copy-done.1), channel_id=1, replica_groups=mesh['yh'=4,'yl'=2,'z'=8,'x'=4,'c'=2] {'yl','z'}, dimensions={0}, use_global_device_ids=true | all-gather | bytes 69632 | tf_op jit(solution)/shard_map/all_gather | solution.py:38
  113.1 4.9 collective-permute-start.2
  127.4 5.4 collective-permute-start.4
  143.5 9.4 %collective-permute-done.8 = f32[512,64]{0,1:T(8,128)S(1)} collective-permute-done((f32[512,64]{0,1:T(8,128)S(1)}, f32[512,64]{0,1:T(8,128)S(1)}, u32[]{:S(2)}, u32[]{:S(2)}) %collective-permute-start.8) | collective-permute-done | bytes 131104 | tf_op jit(solution)/shard_map/ppermute | solution.py:22
  166.0 4.9 collective-permute-start.11
  215.2 5.9 collective-permute-start.17
  238.0 4.9 collective-permute-start.24
  253.8 6.8 %collective-permute-done.26 = f32[2]{0:T(128)S(1)} collective-permute-done((f32[2]{0:T(128)S(1)}, f32[2]{0:T(128)S(1)}, u32[]{:S(2)}, u32[]{:S(2)}) %collective-permute-start.26) | collective-permute-done | bytes 40 | tf_op jit(solution)/shard_map/ppermute | solution.py:22
  291.4 4.9 collective-permute-done.30
  308.9 10.6 %collective-permute-start.35 = (f32[512,64]{0,1:T(8,128)S(1)}, f32[512,64]{0,1:T(8,128)S(1)}, u32[]{:S(2)}, u32[]{:S(2)}) collective-permute-start(f32[512,64]{0,1:T(8,128)S(1)} %add.406), channel_id=1, source_target_pairs={{0,32},{8,40},{16,48},{24,56},{32,0},{40,8},{48,16},{56,24},{1,33}... | collective-permute-start | bytes 393224 | tf_op jit(solution)/shard_map/ppermute | solution.py:22
  335.5 4.9 collective-permute-start.38
  349.6 5.6 collective-permute-start.40
  374.5 9.2 %collective-permute-start.48 = (f32[512,64]{0,1:T(8,128)S(1)}, f32[512,64]{0,1:T(8,128)S(1)}, u32[]{:S(2)}, u32[]{:S(2)}) collective-permute-start(f32[512,64]{0,1:T(8,128)S(1)} %add.422), channel_id=1, source_target_pairs={{0,32},{8,40},{16,48},{24,56},{32,0},{40,8},{48,16},{56,24},{1,33}... | collective-permute-start | bytes 393224 | tf_op jit(solution)/shard_map/ppermute | solution.py:22
  393.4 7.4 %collective-permute-done.44 = f32[2]{0:T(128)S(1)} collective-permute-done((f32[2]{0:T(128)S(1)}, f32[2]{0:T(128)S(1)}, u32[]{:S(2)}, u32[]{:S(2)}) %collective-permute-start.44) | collective-permute-done | bytes 40 | tf_op jit(solution)/shard_map/ppermute | solution.py:22
  427.5 5.0 collective-permute-start.53
  470.9 5.0 collective-permute-start.58
  481.0 5.5 collective-permute-done.61
  488.5 8.8 %collective-permute-done.62 = f32[512,64]{0,1:T(8,128)S(1)} collective-permute-done((f32[512,64]{0,1:T(8,128)S(1)}, f32[512,64]{0,1:T(8,128)S(1)}, u32[]{:S(2)}, u32[]{:S(2)}) %collective-permute-start.62) | collective-permute-done | bytes 131104 | tf_op jit(solution)/shard_map/ppermute | solution.py:22
  510.4 4.9 collective-permute-start.65
  560.6 7.8 %collective-permute-start.71 = (f32[2]{0:T(128)S(1)}, f32[2]{0:T(128)S(1)}, u32[]{:S(2)}, u32[]{:S(2)}) collective-permute-start(f32[2]{0:T(128)S(1)} %add.456), channel_id=1, source_target_pairs={{0,32},{8,40},{16,48},{24,56},{32,0},{40,8},{48,16},{56,24},{1,33}... | collective-permute-start | bytes 32 | tf_op jit(solution)/shard_map/ppermute | solution.py:22
  583.4 4.9 collective-permute-start.78
  600.8 5.2 collective-permute-done.80
  (311 shorter events, 388.2 us)
Async XLA Ops:
  9.1 80.8 %all-to-all-start = ((f32[4,1,65536]{2,1,0:T(1,128)}), f32[4,1,65536]{2,1,0:T(1,128)S(1)}, u32[]{:S(2)}, u32[]{:S(2)}) async-start(f32[4,1,65536]{2,1,0:T(1,128)} %reshape.50), calls=%async_computation | async-start | bytes 2097152 | tf_op jit(solution)/shard_map/all_to_all | solution.py:32
  105.3 27.6 %collective-permute-start.6 = (f32[512,64]{0,1:T(8,128)S(1)}, f32[512,64]{0,1:T(8,128)S(1)}, u32[]{:S(2)}, u32[]{:S(2)}) collective-permute-start(f32[512,64]{0,1:T(8,128)S(1)} %fusion.41), channel_id=1, source_target_pairs={{0,8},{8,0},{16,24},{24,16},{32,40},{40,32},{48,56},{56,48},{1,9},... | collective-permute-start | bytes 393224 | tf_op jit(solution)/shard_map/ppermute | solution.py:22
  127.4 9.7 %collective-permute-start.4 = (f32[256,32]{0,1:T(8,128)S(1)}, f32[256,32]{0,1:T(8,128)S(1)}, u32[]{:S(2)}, u32[]{:S(2)}) collective-permute-start(f32[256,32]{0,1:T(8,128)S(1)} %add.364), channel_id=1, source_target_pairs={{0,256},{128,384},{256,0},{384,128},{1,257},{129,385},{257,1},{385... | collective-permute-start | bytes 98312 | tf_op jit(solution)/shard_map/ppermute | solution.py:22
  140.8 12.1 %collective-permute-start.8 = (f32[512,64]{0,1:T(8,128)S(1)}, f32[512,64]{0,1:T(8,128)S(1)}, u32[]{:S(2)}, u32[]{:S(2)}) collective-permute-start(f32[512,64]{0,1:T(8,128)S(1)} %add.368), channel_id=1, source_target_pairs={{0,32},{8,40},{16,48},{24,56},{32,0},{40,8},{48,16},{56,24},{1,33}... | collective-permute-start | bytes 393224 | tf_op jit(solution)/shard_map/ppermute | solution.py:22
  158.2 26.0 %collective-permute-start.18 = (f32[512,64]{0,1:T(8,128)S(1)}, f32[512,64]{0,1:T(8,128)S(1)}, u32[]{:S(2)}, u32[]{:S(2)}) collective-permute-start(f32[512,64]{0,1:T(8,128)S(1)} %pad_maximum_fusion.2), channel_id=1, source_target_pairs={{0,64},{64,0},{1,65},{65,1},{2,66},{66,2},{3,67},{67,3},{4,68},{68... | collective-permute-start | bytes 393224 | tf_op jit(solution)/shard_map/ppermute | solution.py:22
  180.0 9.7 %collective-permute-start.13 = (f32[256,32]{0,1:T(8,128)S(1)}, f32[256,32]{0,1:T(8,128)S(1)}, u32[]{:S(2)}, u32[]{:S(2)}) collective-permute-start(f32[256,32]{0,1:T(8,128)S(1)} %add.375), channel_id=1, source_target_pairs={{0,256},{128,384},{256,0},{384,128},{1,257},{129,385},{257,1},{385... | collective-permute-start | bytes 98312 | tf_op jit(solution)/shard_map/ppermute | solution.py:22
  184.3 11.5 %collective-permute-start.19 = (f32[512,64]{0,1:T(8,128)S(1)}, f32[512,64]{0,1:T(8,128)S(1)}, u32[]{:S(2)}, u32[]{:S(2)}) collective-permute-start(f32[512,64]{0,1:T(8,128)S(1)} %fusion.40), channel_id=1, source_target_pairs={{0,8},{8,0},{16,24},{24,16},{32,40},{40,32},{48,56},{56,48},{1,9},... | collective-permute-start | bytes 393224 | tf_op jit(solution)/shard_map/ppermute | solution.py:22
  203.6 21.5 %collective-permute-start.21 = (f32[512,64]{0,1:T(8,128)S(1)}, f32[512,64]{0,1:T(8,128)S(1)}, u32[]{:S(2)}, u32[]{:S(2)}) collective-permute-start(f32[512,64]{0,1:T(8,128)S(1)} %add.384), channel_id=1, source_target_pairs={{0,32},{8,40},{16,48},{24,56},{32,0},{40,8},{48,16},{56,24},{1,33}... | collective-permute-start | bytes 393224 | tf_op jit(solution)/shard_map/ppermute | solution.py:22
  272.9 27.5 %collective-permute-start.33 = (f32[512,64]{0,1:T(8,128)S(1)}, f32[512,64]{0,1:T(8,128)S(1)}, u32[]{:S(2)}, u32[]{:S(2)}) collective-permute-start(f32[512,64]{0,1:T(8,128)S(1)} %fusion.39), channel_id=1, source_target_pairs={{0,8},{8,0},{16,24},{24,16},{32,40},{40,32},{48,56},{56,48},{1,9},... | collective-permute-start | bytes 393224 | tf_op jit(solution)/shard_map/ppermute | solution.py:22
  308.9 13.6 %collective-permute-start.35 = (f32[512,64]{0,1:T(8,128)S(1)}, f32[512,64]{0,1:T(8,128)S(1)}, u32[]{:S(2)}, u32[]{:S(2)}) collective-permute-start(f32[512,64]{0,1:T(8,128)S(1)} %add.406), channel_id=1, source_target_pairs={{0,32},{8,40},{16,48},{24,56},{32,0},{40,8},{48,16},{56,24},{1,33}... | collective-permute-start | bytes 393224 | tf_op jit(solution)/shard_map/ppermute | solution.py:22
  327.8 27.4 %collective-permute-start.45 = (f32[512,64]{0,1:T(8,128)S(1)}, f32[512,64]{0,1:T(8,128)S(1)}, u32[]{:S(2)}, u32[]{:S(2)}) collective-permute-start(f32[512,64]{0,1:T(8,128)S(1)} %pad_maximum_fusion.4), channel_id=1, source_target_pairs={{0,64},{64,0},{1,65},{65,1},{2,66},{66,2},{3,67},{67,3},{4,68},{68... | collective-permute-start | bytes 393224 | tf_op jit(solution)/shard_map/ppermute | solution.py:22
  349.6 9.7 %collective-permute-start.40 = (f32[256,32]{0,1:T(8,128)S(1)}, f32[256,32]{0,1:T(8,128)S(1)}, u32[]{:S(2)}, u32[]{:S(2)}) collective-permute-start(f32[256,32]{0,1:T(8,128)S(1)} %add.413), channel_id=1, source_target_pairs={{0,256},{128,384},{256,0},{384,128},{1,257},{129,385},{257,1},{385... | collective-permute-start | bytes 98312 | tf_op jit(solution)/shard_map/ppermute | solution.py:22
  355.2 10.9 %collective-permute-start.46 = (f32[512,64]{0,1:T(8,128)S(1)}, f32[512,64]{0,1:T(8,128)S(1)}, u32[]{:S(2)}, u32[]{:S(2)}) collective-permute-start(f32[512,64]{0,1:T(8,128)S(1)} %fusion.38), channel_id=1, source_target_pairs={{0,8},{8,0},{16,24},{24,16},{32,40},{40,32},{48,56},{56,48},{1,9},... | collective-permute-start | bytes 393224 | tf_op jit(solution)/shard_map/ppermute | solution.py:22
  369.5 14.2 %collective-permute-start.42 = (f32[2]{0:T(128)S(1)}, f32[2]{0:T(128)S(1)}, u32[]{:S(2)}, u32[]{:S(2)}) collective-permute-start(f32[2]{0:T(128)S(1)} %fusion.125), channel_id=1, source_target_pairs={{0,8},{8,0},{16,24},{24,16},{32,40},{40,32},{48,56},{56,48},{1,9},... | collective-permute-start | bytes 32 | tf_op jit(solution)/shard_map/ppermute | solution.py:22
  374.5 26.9 %collective-permute-start.48 = (f32[512,64]{0,1:T(8,128)S(1)}, f32[512,64]{0,1:T(8,128)S(1)}, u32[]{:S(2)}, u32[]{:S(2)}) collective-permute-start(f32[512,64]{0,1:T(8,128)S(1)} %add.422), channel_id=1, source_target_pairs={{0,32},{8,40},{16,48},{24,56},{32,0},{40,8},{48,16},{56,24},{1,33}... | collective-permute-start | bytes 393224 | tf_op jit(solution)/shard_map/ppermute | solution.py:22
  449.2 26.7 %collective-permute-start.60 = (f32[512,64]{0,1:T(8,128)S(1)}, f32[512,64]{0,1:T(8,128)S(1)}, u32[]{:S(2)}, u32[]{:S(2)}) collective-permute-start(f32[512,64]{0,1:T(8,128)S(1)} %fusion.37), channel_id=1, source_target_pairs={{0,8},{8,0},{16,24},{24,16},{32,40},{40,32},{48,56},{56,48},{1,9},... | collective-permute-start | bytes 393224 | tf_op jit(solution)/shard_map/ppermute | solution.py:22
  470.9 10.1 %collective-permute-start.58 = (f32[256,32]{0,1:T(8,128)S(1)}, f32[256,32]{0,1:T(8,128)S(1)}, u32[]{:S(2)}, u32[]{:S(2)}) collective-permute-start(f32[256,32]{0,1:T(8,128)S(1)} %add.440), channel_id=1, source_target_pairs={{0,256},{128,384},{256,0},{384,128},{1,257},{129,385},{257,1},{385... | collective-permute-start | bytes 98312 | tf_op jit(solution)/shard_map/ppermute | solution.py:22
  475.9 10.6 %collective-permute-start.61 = (f32[512,64]{0,1:T(8,128)S(1)}, f32[512,64]{0,1:T(8,128)S(1)}, u32[]{:S(2)}, u32[]{:S(2)}) collective-permute-start(f32[512,64]{0,1:T(8,128)S(1)} %add.443), channel_id=1, source_target_pairs={{0,16},{8,24},{16,0},{24,8},{32,48},{40,56},{48,32},{56,40},{1,17}... | collective-permute-start | bytes 393224 | tf_op jit(solution)/shard_map/ppermute | solution.py:22
  486.5 10.8 %collective-permute-start.62 = (f32[512,64]{0,1:T(8,128)S(1)}, f32[512,64]{0,1:T(8,128)S(1)}, u32[]{:S(2)}, u32[]{:S(2)}) collective-permute-start(f32[512,64]{0,1:T(8,128)S(1)} %add.444), channel_id=1, source_target_pairs={{0,32},{8,40},{16,48},{24,56},{32,0},{40,8},{48,16},{56,24},{1,33}... | collective-permute-start | bytes 393224 | tf_op jit(solution)/shard_map/ppermute | solution.py:22
  502.7 26.0 %collective-permute-start.72 = (f32[512,64]{0,1:T(8,128)S(1)}, f32[512,64]{0,1:T(8,128)S(1)}, u32[]{:S(2)}, u32[]{:S(2)}) collective-permute-start(f32[512,64]{0,1:T(8,128)S(1)} %pad_maximum_fusion.6), channel_id=1, source_target_pairs={{0,64},{64,0},{1,65},{65,1},{2,66},{66,2},{3,67},{67,3},{4,68},{68... | collective-permute-start | bytes 393224 | tf_op jit(solution)/shard_map/ppermute | solution.py:22
  524.4 9.7 %collective-permute-start.67 = (f32[256,32]{0,1:T(8,128)S(1)}, f32[256,32]{0,1:T(8,128)S(1)}, u32[]{:S(2)}, u32[]{:S(2)}) collective-permute-start(f32[256,32]{0,1:T(8,128)S(1)} %add.451), channel_id=1, source_target_pairs={{0,256},{128,384},{256,0},{384,128},{1,257},{129,385},{257,1},{385... | collective-permute-start | bytes 98312 | tf_op jit(solution)/shard_map/ppermute | solution.py:22
  528.7 12.0 %collective-permute-start.73 = (f32[512,64]{0,1:T(8,128)S(1)}, f32[512,64]{0,1:T(8,128)S(1)}, u32[]{:S(2)}, u32[]{:S(2)}) collective-permute-start(f32[512,64]{0,1:T(8,128)S(1)} %fusion.36), channel_id=1, source_target_pairs={{0,8},{8,0},{16,24},{24,16},{32,40},{40,32},{48,56},{56,48},{1,9},... | collective-permute-start | bytes 393224 | tf_op jit(solution)/shard_map/ppermute | solution.py:22
  540.8 10.1 %collective-permute-start.74 = (f32[512,64]{0,1:T(8,128)S(1)}, f32[512,64]{0,1:T(8,128)S(1)}, u32[]{:S(2)}, u32[]{:S(2)}) collective-permute-start(f32[512,64]{0,1:T(8,128)S(1)} %add.459), channel_id=1, source_target_pairs={{0,16},{8,24},{16,0},{24,8},{32,48},{40,56},{48,32},{56,40},{1,17}... | collective-permute-start | bytes 393224 | tf_op jit(solution)/shard_map/ppermute | solution.py:22
  550.9 19.6 %collective-permute-start.75 = (f32[512,64]{0,1:T(8,128)S(1)}, f32[512,64]{0,1:T(8,128)S(1)}, u32[]{:S(2)}, u32[]{:S(2)}) collective-permute-start(f32[512,64]{0,1:T(8,128)S(1)} %add.460), channel_id=1, source_target_pairs={{0,32},{8,40},{16,48},{24,56},{32,0},{40,8},{48,16},{56,24},{1,33}... | collective-permute-start | bytes 393224 | tf_op jit(solution)/shard_map/ppermute | solution.py:22
  (60 other events, 439.5 us)
where the time goes:
time: 614 us; the launch traced here: 611 us
  starting transfers between devices  281 us (46%)
  waiting for transfers between devices  177 us (29%)
  blocking collectives  73.5 us (12%)
  other arithmetic  39.6 us (6%)
  matrix products  16.2 us (3%)
  local copies, waits for them, and re-layouts  13.5 us (2%)
  between operations  9.89 us (2%)
    ppermute x81, starting transfers between devices, doubling_sum(): value = value + lax.ppermute(value, name, pairs)  274 us
    ppermute x81, waiting for transfers between devices, doubling_sum(): value = value + lax.ppermute(value, name, pairs)  177 us
    all_gather x1, blocking collectives, per_device(): f_zero = lax.all_gather(freqs, ROW_GROUP, axis=0, tiled=True)  40.7 us
    all_gather x1, blocking collectives, per_device(): q_zero = lax.all_gather(q_own, 'yh', axis=0, tiled=True)  32.8 us
    add x75, other arithmetic, doubling_sum(): value = value + lax.ppermute(value, name, pairs)  16.6 us
  transfers between devices with their start and end apart: 82, of which 57 were waited for; matrix products, arithmetic and copies ran while one was open for 3% of the time, Pallas kernels for 0%

commit v1 on v0

--- a/solution.py
+++ b/solution.py
@@ -35,7 +35,9 @@
     own_snps = freqs.shape[0]
     q_own = ancestry / jnp.sum(ancestry, axis=1, keepdims=True)
     q_zero = lax.all_gather(q_own, "yh", axis=0, tiled=True)
-    f_zero = lax.all_gather(freqs, ROW_GROUP, axis=0, tiled=True)
+    f_zero = jnp.concatenate(
+        lax.all_to_all(jnp.stack([freqs] * lax.axis_size(ROW_GROUP)), ROW_GROUP, 0, 0), axis=0
+    )
 
     def em_map(q_rows, f_state):
         prob = jnp.dot(q_rows, f_state.T, precision=high, preferred_element_type=jnp.float32)

time: 614 us -> 594 us (0.967)
  blocking collectives: 73.5 us -> 31.9 us
  starting transfers between devices: 281 us -> 307 us
  waiting for transfers between devices: 177 us -> 169 us
    all_gather x1 -> x0, blocking collectives: 40.7 us -> none  [per_device(): f_zero = lax.all_gather(freqs, ROW_GROUP, axis=0, tiled=True)]
    ppermute x81, starting transfers between devices: 274 us -> 288 us  [doubling_sum(): value = value + lax.ppermute(value, name, pairs)]
    all_to_all x0 -> x1, starting transfers between devices: none -> 11.8 us  [per_device(): lax.all_to_all(jnp.stack([freqs] * lax.axis_size(ROW_GROUP)), ROW_GROUP,...]
    ppermute x81, waiting for transfers between devices: 177 us -> 169 us  [doubling_sum(): value = value + lax.ppermute(value, name, pairs)]
  transfers between devices with their start and end apart: 82 -> 83, of which waited for: 57 -> 56; matrix products, arithmetic and copies ran while one was open for 3% -> 5% of each run, Pallas kernels for 0% -> 0%
where the time goes in v1:
time: 594 us; the launch traced here: 590 us
  starting transfers between devices  307 us (52%)
  waiting for transfers between devices  169 us (28%)
  other arithmetic  41.2 us (7%)
  blocking collectives  31.9 us (5%)
  matrix products  16.2 us (3%)
  local copies, waits for them, and re-layouts  14.5 us (2%)
  between operations  10.1 us (2%)
    ppermute x81, starting transfers between devices, doubling_sum(): value = value + lax.ppermute(value, name, pairs)  288 us
    ppermute x81, waiting for transfers between devices, doubling_sum(): value = value + lax.ppermute(value, name, pairs)  169 us
    all_gather x1, blocking collectives, per_device(): q_zero = lax.all_gather(q_own, 'yh', axis=0, tiled=True)  31.9 us
    add x75, other arithmetic, doubling_sum(): value = value + lax.ppermute(value, name, pairs)  17.1 us
  transfers between devices with their start and end apart: 83, of which 56 were waited for; matrix products, arithmetic and copies ran while one was open for 5% of the time, Pallas kernels for 0%

profile of v1, /device:TPU:56, one launch (start us, length us, event | category | flops | bytes accessed | tf_op | source)
XLA Modules:
  0.0 590.5 jit_solution(14750352266712451854)
XLA Ops:
  2.3 11.8 %all-to-all-start.1 = ((f32[16,1,1024]{2,1,0:T(1,128)}), f32[16,1,1024]{2,1,0:T(1,128)S(1)}, u32[]{:S(2)}, u32[]{:S(2)}) async-start(f32[16,1,1024]{2,1,0:T(1,128)} %reshape.56), calls=%async_computation.1 | async-start | bytes 131072 | tf_op jit(solution)/shard_map/all_to_all | solution.py:39
  21.5 7.0 %all-to-all-start = ((f32[4,1,65536]{2,1,0:T(1,128)}), f32[4,1,65536]{2,1,0:T(1,128)S(1)}, u32[]{:S(2)}, u32[]{:S(2)}) async-start(f32[4,1,65536]{2,1,0:T(1,128)} %reshape.58), calls=%async_computation | async-start | bytes 2097152 | tf_op jit(solution)/shard_map/all_to_all | solution.py:32
  28.5 31.9 %all-gather = f32[4,64,32]{1,2,0:T(8,128)S(1)} all-gather(f32[1,64,32]{1,2,0:T(8,128)S(1)} %divide_bitcast_fusion), channel_id=1, replica_groups=mesh['yh'=4,'yl'=2,'z'=8,'x'=4,'c'=2] {'yh'}, dimensions={0}, use_global_device_ids=true | all-gather | bytes 40960 | tf_op jit(solution)/shard_map/all_gather | solution.py:37
  87.4 4.9 collective-permute-start.2
  115.1 9.2 %collective-permute-start.8 = (f32[512,64]{0,1:T(8,128)S(1)}, f32[512,64]{0,1:T(8,128)S(1)}, u32[]{:S(2)}, u32[]{:S(2)}) collective-permute-start(f32[512,64]{0,1:T(8,128)S(1)} %add.368), channel_id=1, source_target_pairs={{0,32},{8,40},{16,48},{24,56},{32,0},{40,8},{48,16},{56,24},{1,33}... | collective-permute-start | bytes 393224 | tf_op jit(solution)/shard_map/ppermute | solution.py:22
  140.4 4.9 collective-permute-start.11
  177.9 9.3 %collective-permute-start.21 = (f32[512,64]{0,1:T(8,128)S(1)}, f32[512,64]{0,1:T(8,128)S(1)}, u32[]{:S(2)}, u32[]{:S(2)}) collective-permute-start(f32[512,64]{0,1:T(8,128)S(1)} %add.384), channel_id=1, source_target_pairs={{0,32},{8,40},{16,48},{24,56},{32,0},{40,8},{48,16},{56,24},{1,33}... | collective-permute-start | bytes 393224 | tf_op jit(solution)/shard_map/ppermute | solution.py:22
  196.9 7.4 %collective-permute-done.17 = f32[2]{0:T(128)S(1)} collective-permute-done((f32[2]{0:T(128)S(1)}, f32[2]{0:T(128)S(1)}, u32[]{:S(2)}, u32[]{:S(2)}) %collective-permute-start.17) | collective-permute-done | bytes 40 | tf_op jit(solution)/shard_map/ppermute | solution.py:22
  218.2 4.9 collective-permute-start.24
  231.5 5.2 collective-permute-start.26
  261.0 4.9 collective-permute-start.29
  275.0 5.2 collective-permute-start.31
  284.7 5.5 collective-permute-done.34
  292.2 8.8 %collective-permute-done.35 = f32[512,64]{0,1:T(8,128)S(1)} collective-permute-done((f32[512,64]{0,1:T(8,128)S(1)}, f32[512,64]{0,1:T(8,128)S(1)}, u32[]{:S(2)}, u32[]{:S(2)}) %collective-permute-start.35) | collective-permute-done | bytes 131104 | tf_op jit(solution)/shard_map/ppermute | solution.py:22
  314.1 4.9 collective-permute-start.38
  364.3 7.8 %collective-permute-start.44 = (f32[2]{0:T(128)S(1)}, f32[2]{0:T(128)S(1)}, u32[]{:S(2)}, u32[]{:S(2)}) collective-permute-start(f32[2]{0:T(128)S(1)} %add.418), channel_id=1, source_target_pairs={{0,32},{8,40},{16,48},{24,56},{32,0},{40,8},{48,16},{56,24},{1,33}... | collective-permute-start | bytes 32 | tf_op jit(solution)/shard_map/ppermute | solution.py:22
  387.5 4.9 collective-permute-start.51
  405.0 5.1 collective-permute-done.53
  430.3 4.9 collective-permute-start.56
  456.7 10.7 %collective-permute-start.62 = (f32[512,64]{0,1:T(8,128)S(1)}, f32[512,64]{0,1:T(8,128)S(1)}, u32[]{:S(2)}, u32[]{:S(2)}) collective-permute-start(f32[512,64]{0,1:T(8,128)S(1)} %add.444), channel_id=1, source_target_pairs={{0,32},{8,40},{16,48},{24,56},{32,0},{40,8},{48,16},{56,24},{1,33}... | collective-permute-start | bytes 393224 | tf_op jit(solution)/shard_map/ppermute | solution.py:22
  483.4 4.9 collective-permute-start.65
  522.9 9.2 %collective-permute-start.75 = (f32[512,64]{0,1:T(8,128)S(1)}, f32[512,64]{0,1:T(8,128)S(1)}, u32[]{:S(2)}, u32[]{:S(2)}) collective-permute-start(f32[512,64]{0,1:T(8,128)S(1)} %add.460), channel_id=1, source_target_pairs={{0,32},{8,40},{16,48},{24,56},{32,0},{40,8},{48,16},{56,24},{1,33}... | collective-permute-start | bytes 393224 | tf_op jit(solution)/shard_map/ppermute | solution.py:22
  541.7 7.4 %collective-permute-done.71 = f32[2]{0:T(128)S(1)} collective-permute-done((f32[2]{0:T(128)S(1)}, f32[2]{0:T(128)S(1)}, u32[]{:S(2)}, u32[]{:S(2)}) %collective-permute-start.71) | collective-permute-done | bytes 40 | tf_op jit(solution)/shard_map/ppermute | solution.py:22
  563.0 4.9 collective-permute-start.78
  (318 shorter events, 394.6 us)
Async XLA Ops:
  2.3 19.2 %all-to-all-start.1 = ((f32[16,1,1024]{2,1,0:T(1,128)}), f32[16,1,1024]{2,1,0:T(1,128)S(1)}, u32[]{:S(2)}, u32[]{:S(2)}) async-start(f32[16,1,1024]{2,1,0:T(1,128)} %reshape.56), calls=%async_computation.1 | async-start | bytes 131072 | tf_op jit(solution)/shard_map/all_to_all | solution.py:39
  21.5 40.8 %all-to-all-start = ((f32[4,1,65536]{2,1,0:T(1,128)}), f32[4,1,65536]{2,1,0:T(1,128)S(1)}, u32[]{:S(2)}, u32[]{:S(2)}) async-start(f32[4,1,65536]{2,1,0:T(1,128)} %reshape.58), calls=%async_computation | async-start | bytes 2097152 | tf_op jit(solution)/shard_map/all_to_all | solution.py:32
  77.7 28.3 %collective-permute-start.6 = (f32[512,64]{0,1:T(8,128)S(1)}, f32[512,64]{0,1:T(8,128)S(1)}, u32[]{:S(2)}, u32[]{:S(2)}) collective-permute-start(f32[512,64]{0,1:T(8,128)S(1)} %fusion.40), channel_id=1, source_target_pairs={{0,8},{8,0},{16,24},{24,16},{32,40},{40,32},{48,56},{56,48},{1,9},... | collective-permute-start | bytes 393224 | tf_op jit(solution)/shard_map/ppermute | solution.py:22
  115.1 12.0 %collective-permute-start.8 = (f32[512,64]{0,1:T(8,128)S(1)}, f32[512,64]{0,1:T(8,128)S(1)}, u32[]{:S(2)}, u32[]{:S(2)}) collective-permute-start(f32[512,64]{0,1:T(8,128)S(1)} %add.368), channel_id=1, source_target_pairs={{0,32},{8,40},{16,48},{24,56},{32,0},{40,8},{48,16},{56,24},{1,33}... | collective-permute-start | bytes 393224 | tf_op jit(solution)/shard_map/ppermute | solution.py:22
  132.4 26.9 %collective-permute-start.18 = (f32[512,64]{0,1:T(8,128)S(1)}, f32[512,64]{0,1:T(8,128)S(1)}, u32[]{:S(2)}, u32[]{:S(2)}) collective-permute-start(f32[512,64]{0,1:T(8,128)S(1)} %pad_maximum_fusion.2), channel_id=1, source_target_pairs={{0,64},{64,0},{1,65},{65,1},{2,66},{66,2},{3,67},{67,3},{4,68},{68... | collective-permute-start | bytes 393224 | tf_op jit(solution)/shard_map/ppermute | solution.py:22
  159.4 10.4 %collective-permute-start.19 = (f32[512,64]{0,1:T(8,128)S(1)}, f32[512,64]{0,1:T(8,128)S(1)}, u32[]{:S(2)}, u32[]{:S(2)}) collective-permute-start(f32[512,64]{0,1:T(8,128)S(1)} %fusion.39), channel_id=1, source_target_pairs={{0,8},{8,0},{16,24},{24,16},{32,40},{40,32},{48,56},{56,48},{1,9},... | collective-permute-start | bytes 393224 | tf_op jit(solution)/shard_map/ppermute | solution.py:22
  173.2 14.1 %collective-permute-start.15 = (f32[2]{0:T(128)S(1)}, f32[2]{0:T(128)S(1)}, u32[]{:S(2)}, u32[]{:S(2)}) collective-permute-start(f32[2]{0:T(128)S(1)} %fusion.127), channel_id=1, source_target_pairs={{0,8},{8,0},{16,24},{24,16},{32,40},{40,32},{48,56},{56,48},{1,9},... | collective-permute-start | bytes 32 | tf_op jit(solution)/shard_map/ppermute | solution.py:22
  177.9 26.9 %collective-permute-start.21 = (f32[512,64]{0,1:T(8,128)S(1)}, f32[512,64]{0,1:T(8,128)S(1)}, u32[]{:S(2)}, u32[]{:S(2)}) collective-permute-start(f32[512,64]{0,1:T(8,128)S(1)} %add.384), channel_id=1, source_target_pairs={{0,32},{8,40},{16,48},{24,56},{32,0},{40,8},{48,16},{56,24},{1,33}... | collective-permute-start | bytes 393224 | tf_op jit(solution)/shard_map/ppermute | solution.py:22
  253.2 26.9 %collective-permute-start.33 = (f32[512,64]{0,1:T(8,128)S(1)}, f32[512,64]{0,1:T(8,128)S(1)}, u32[]{:S(2)}, u32[]{:S(2)}) collective-permute-start(f32[512,64]{0,1:T(8,128)S(1)} %fusion.38), channel_id=1, source_target_pairs={{0,8},{8,0},{16,24},{24,16},{32,40},{40,32},{48,56},{56,48},{1,9},... | collective-permute-start | bytes 393224 | tf_op jit(solution)/shard_map/ppermute | solution.py:22
  275.0 9.7 %collective-permute-start.31 = (f32[256,32]{0,1:T(8,128)S(1)}, f32[256,32]{0,1:T(8,128)S(1)}, u32[]{:S(2)}, u32[]{:S(2)}) collective-permute-start(f32[256,32]{0,1:T(8,128)S(1)} %add.402), channel_id=1, source_target_pairs={{0,256},{128,384},{256,0},{384,128},{1,257},{129,385},{257,1},{385... | collective-permute-start | bytes 98312 | tf_op jit(solution)/shard_map/ppermute | solution.py:22
  280.2 10.0 %collective-permute-start.34 = (f32[512,64]{0,1:T(8,128)S(1)}, f32[512,64]{0,1:T(8,128)S(1)}, u32[]{:S(2)}, u32[]{:S(2)}) collective-permute-start(f32[512,64]{0,1:T(8,128)S(1)} %add.405), channel_id=1, source_target_pairs={{0,16},{8,24},{16,0},{24,8},{32,48},{40,56},{48,32},{56,40},{1,17}... | collective-permute-start | bytes 393224 | tf_op jit(solution)/shard_map/ppermute | solution.py:22
  290.2 10.8 %collective-permute-start.35 = (f32[512,64]{0,1:T(8,128)S(1)}, f32[512,64]{0,1:T(8,128)S(1)}, u32[]{:S(2)}, u32[]{:S(2)}) collective-permute-start(f32[512,64]{0,1:T(8,128)S(1)} %add.406), channel_id=1, source_target_pairs={{0,32},{8,40},{16,48},{24,56},{32,0},{40,8},{48,16},{56,24},{1,33}... | collective-permute-start | bytes 393224 | tf_op jit(solution)/shard_map/ppermute | solution.py:22
  306.3 26.4 %collective-permute-start.45 = (f32[512,64]{0,1:T(8,128)S(1)}, f32[512,64]{0,1:T(8,128)S(1)}, u32[]{:S(2)}, u32[]{:S(2)}) collective-permute-start(f32[512,64]{0,1:T(8,128)S(1)} %pad_maximum_fusion.4), channel_id=1, source_target_pairs={{0,64},{64,0},{1,65},{65,1},{2,66},{66,2},{3,67},{67,3},{4,68},{68... | collective-permute-start | bytes 393224 | tf_op jit(solution)/shard_map/ppermute | solution.py:22
  328.1 9.7 %collective-permute-start.40 = (f32[256,32]{0,1:T(8,128)S(1)}, f32[256,32]{0,1:T(8,128)S(1)}, u32[]{:S(2)}, u32[]{:S(2)}) collective-permute-start(f32[256,32]{0,1:T(8,128)S(1)} %add.413), channel_id=1, source_target_pairs={{0,256},{128,384},{256,0},{384,128},{1,257},{129,385},{257,1},{385... | collective-permute-start | bytes 98312 | tf_op jit(solution)/shard_map/ppermute | solution.py:22
  332.7 11.9 %collective-permute-start.46 = (f32[512,64]{0,1:T(8,128)S(1)}, f32[512,64]{0,1:T(8,128)S(1)}, u32[]{:S(2)}, u32[]{:S(2)}) collective-permute-start(f32[512,64]{0,1:T(8,128)S(1)} %fusion.37), channel_id=1, source_target_pairs={{0,8},{8,0},{16,24},{24,16},{32,40},{40,32},{48,56},{56,48},{1,9},... | collective-permute-start | bytes 393224 | tf_op jit(solution)/shard_map/ppermute | solution.py:22
  344.7 10.0 %collective-permute-start.47 = (f32[512,64]{0,1:T(8,128)S(1)}, f32[512,64]{0,1:T(8,128)S(1)}, u32[]{:S(2)}, u32[]{:S(2)}) collective-permute-start(f32[512,64]{0,1:T(8,128)S(1)} %add.421), channel_id=1, source_target_pairs={{0,16},{8,24},{16,0},{24,8},{32,48},{40,56},{48,32},{56,40},{1,17}... | collective-permute-start | bytes 393224 | tf_op jit(solution)/shard_map/ppermute | solution.py:22
  354.7 19.5 %collective-permute-start.48 = (f32[512,64]{0,1:T(8,128)S(1)}, f32[512,64]{0,1:T(8,128)S(1)}, u32[]{:S(2)}, u32[]{:S(2)}) collective-permute-start(f32[512,64]{0,1:T(8,128)S(1)} %add.422), channel_id=1, source_target_pairs={{0,32},{8,40},{16,48},{24,56},{32,0},{40,8},{48,16},{56,24},{1,33}... | collective-permute-start | bytes 393224 | tf_op jit(solution)/shard_map/ppermute | solution.py:22
  422.5 26.4 %collective-permute-start.60 = (f32[512,64]{0,1:T(8,128)S(1)}, f32[512,64]{0,1:T(8,128)S(1)}, u32[]{:S(2)}, u32[]{:S(2)}) collective-permute-start(f32[512,64]{0,1:T(8,128)S(1)} %fusion.36), channel_id=1, source_target_pairs={{0,8},{8,0},{16,24},{24,16},{32,40},{40,32},{48,56},{56,48},{1,9},... | collective-permute-start | bytes 393224 | tf_op jit(solution)/shard_map/ppermute | solution.py:22
  456.7 13.6 %collective-permute-start.62 = (f32[512,64]{0,1:T(8,128)S(1)}, f32[512,64]{0,1:T(8,128)S(1)}, u32[]{:S(2)}, u32[]{:S(2)}) collective-permute-start(f32[512,64]{0,1:T(8,128)S(1)} %add.444), channel_id=1, source_target_pairs={{0,32},{8,40},{16,48},{24,56},{32,0},{40,8},{48,16},{56,24},{1,33}... | collective-permute-start | bytes 393224 | tf_op jit(solution)/shard_map/ppermute | solution.py:22
  475.6 26.6 %collective-permute-start.72 = (f32[512,64]{0,1:T(8,128)S(1)}, f32[512,64]{0,1:T(8,128)S(1)}, u32[]{:S(2)}, u32[]{:S(2)}) collective-permute-start(f32[512,64]{0,1:T(8,128)S(1)} %pad_maximum_fusion.6), channel_id=1, source_target_pairs={{0,64},{64,0},{1,65},{65,1},{2,66},{66,2},{3,67},{67,3},{4,68},{68... | collective-permute-start | bytes 393224 | tf_op jit(solution)/shard_map/ppermute | solution.py:22
  497.4 10.0 %collective-permute-start.67 = (f32[256,32]{0,1:T(8,128)S(1)}, f32[256,32]{0,1:T(8,128)S(1)}, u32[]{:S(2)}, u32[]{:S(2)}) collective-permute-start(f32[256,32]{0,1:T(8,128)S(1)} %add.451), channel_id=1, source_target_pairs={{0,256},{128,384},{256,0},{384,128},{1,257},{129,385},{257,1},{385... | collective-permute-start | bytes 98312 | tf_op jit(solution)/shard_map/ppermute | solution.py:22
  502.3 11.4 %collective-permute-start.73 = (f32[512,64]{0,1:T(8,128)S(1)}, f32[512,64]{0,1:T(8,128)S(1)}, u32[]{:S(2)}, u32[]{:S(2)}) collective-permute-start(f32[512,64]{0,1:T(8,128)S(1)} %fusion.35), channel_id=1, source_target_pairs={{0,8},{8,0},{16,24},{24,16},{32,40},{40,32},{48,56},{56,48},{1,9},... | collective-permute-start | bytes 393224 | tf_op jit(solution)/shard_map/ppermute | solution.py:22
  517.8 14.3 %collective-permute-start.69 = (f32[2]{0:T(128)S(1)}, f32[2]{0:T(128)S(1)}, u32[]{:S(2)}, u32[]{:S(2)}) collective-permute-start(f32[2]{0:T(128)S(1)} %fusion.123), channel_id=1, source_target_pairs={{0,8},{8,0},{16,24},{24,16},{32,40},{40,32},{48,56},{56,48},{1,9},... | collective-permute-start | bytes 32 | tf_op jit(solution)/shard_map/ppermute | solution.py:22
  522.9 26.8 %collective-permute-start.75 = (f32[512,64]{0,1:T(8,128)S(1)}, f32[512,64]{0,1:T(8,128)S(1)}, u32[]{:S(2)}, u32[]{:S(2)}) collective-permute-start(f32[512,64]{0,1:T(8,128)S(1)} %add.460), channel_id=1, source_target_pairs={{0,32},{8,40},{16,48},{24,56},{32,0},{40,8},{48,16},{56,24},{1,33}... | collective-permute-start | bytes 393224 | tf_op jit(solution)/shard_map/ppermute | solution.py:22
  (61 other events, 426.8 us)
